TPU v7x, 256 devices: a whole 4x4x8 slice. The times are simulated.
256 devices in a mesh: dp: 16 (over z_lo, y, core), expert: 16 (over x, z_hi).
Axes of the slice: x: 4, y: 4, z: 8 (z_hi: 4, z_lo: 2; z = z_hi * 2 + z_lo), core: 2. Of those that a mesh axis runs over, the one named last changes fastest.
Arguments:
- tokens: bfloat16 [32768, 2048], P(('dp', 'expert')), may hold values from -6 to 6
- cotangent: bfloat16 [32768, 2048], P(('dp', 'expert')), may hold values from -6 to 6
- hot_mask: int32 [32768], P(('dp', 'expert')), may hold values 0 or 1
- hot_gate: float32 [32768], P(('dp', 'expert')), may hold values from 0.2 to 1
- cold_ids: int32 [32768, 1], P(('dp', 'expert')), may hold values from 0 to 7; in each aligned block of 128 rows (0 to 127, 128 to 255, ...) at most 20 rows name the same one
- cold_gate: float32 [32768, 1], P(('dp', 'expert')), may hold values from 0.2 to 1
- hot_in: bfloat16 [2, 704, 2048], P(None, 'dp'), may hold values from -0.125 to 0.125
- hot_down: bfloat16 [704, 2048], P('dp'), may hold values from -0.21875 to 0.21875
- cold_in: bfloat16 [2, 5632, 2048], P(None, 'expert'), may hold values from -0.125 to 0.125
- cold_down: bfloat16 [5632, 2048], P('expert'), may hold values from -0.21875 to 0.21875
Outputs:
- mixed: bfloat16 [32768, 2048], P(('dp', 'expert'))
- input_grad: bfloat16 [32768, 2048], P(('dp', 'expert'))
- hot_grad_in: float32 [2, 704, 2048], P(None, 'dp', 'expert')
- hot_grad_down: float32 [704, 2048], P('dp', 'expert')
- cold_grad_in: bfloat16 [16, 2, 5632, 2048], P('dp', None, 'expert')
- cold_grad_down: bfloat16 [16, 5632, 2048], P('dp', 'expert')
Inputs may be any that keep to these rules, and one draw needn't show every extreme that they name: `cold_ids`: in each device's block of 128 rows no cold expert is chosen by more than 20 rows, and in every draw some device's block chooses some cold expert exactly 20 times.
All inputs are finite; a program needn't handle non-finite values. No bound on the sum of `hot_mask` on one device may be relied on, other than what follows from the above.
Results may differ from a plain program's by a relative error of at most 0.0059.
Values may be sent and summed in bfloat16 or wider, within the bound.
No kernel may reach another device: no remote copies, remote signals or barrier semaphores. Data moves between devices by JAX's collectives and lax.ppermute only.
A program may use at most 128 MiB of HBM per device.

v0:
```python
import math
import jax
import jax.numpy as jnp
from jax import lax
from jax.sharding import PartitionSpec as P


def passed_along(block, axis, distance):
    devices = range(lax.axis_size(axis))
    route = [((i - distance) % len(devices), i) for i in devices]
    return lax.ppermute(block, axis, route)


def silu_parts(values):
    sigmoid_val = jax.nn.sigmoid(values)
    return (values * sigmoid_val, sigmoid_val * (1.0 + values * (1.0 - sigmoid_val)))


def pass_weights(weights):
    return passed_along(weights, "dp", 1)


def pass_grads(carried):
    return passed_along(carried, "dp", 1)


def hot_terms(tokens, cotangent, hot_weight, weights):
    pre_act = jnp.einsum("td,kud->ktu", tokens, weights[:2], preferred_element_type=jnp.float32)
    silu_out, silu_slope = silu_parts(pre_act[0])
    hidden = (hot_weight[:, None] * silu_out * pre_act[1]).astype(jnp.bfloat16)
    out_part = jnp.dot(hidden, weights[2], preferred_element_type=jnp.float32)
    back_proj = jnp.einsum("td,ud->tu", cotangent, weights[2], preferred_element_type=jnp.float32)
    hidden_grad = hot_weight[:, None] * back_proj
    pre_grad = jnp.stack([hidden_grad * pre_act[1] * silu_slope, hidden_grad * silu_out]).astype(
        jnp.bfloat16
    )
    dx_part = jnp.einsum("ktu,kud->td", pre_grad, weights[:2], preferred_element_type=jnp.float32)
    grad_in = jnp.einsum("ktu,td->kud", pre_grad, tokens, preferred_element_type=jnp.float32)
    grad_down = jnp.einsum("tu,td->ud", hidden, cotangent, preferred_element_type=jnp.float32)
    return (out_part, dx_part, jnp.concatenate([grad_in, grad_down[None]], axis=0))


def cold_terms(row_block, cold_in, cold_down):
    pre_act = jnp.einsum("rd,kud->kru", row_block[0], cold_in, preferred_element_type=jnp.float32)
    silu_out, silu_slope = silu_parts(pre_act[0])
    hidden = (silu_out * pre_act[1]).astype(jnp.bfloat16)
    out_part = jnp.dot(hidden, cold_down, preferred_element_type=jnp.float32).astype(jnp.bfloat16)
    back_proj = jnp.einsum("rd,ud->ru", row_block[1], cold_down, preferred_element_type=jnp.float32)
    pre_grad = jnp.stack([back_proj * pre_act[1] * silu_slope, back_proj * silu_out]).astype(
        jnp.bfloat16
    )
    dx_part = jnp.einsum(
        "kru,kud->rd", pre_grad, cold_in, preferred_element_type=jnp.float32
    ).astype(jnp.bfloat16)
    grad_in = jnp.einsum("kru,rd->kud", pre_grad, row_block[0], preferred_element_type=jnp.float32)
    grad_down = jnp.einsum("ru,rd->ud", hidden, row_block[1], preferred_element_type=jnp.float32)
    return (out_part, dx_part, grad_in, grad_down)


def body(
    tokens, cotangent, hot_mask, hot_gate, cold_ids, cold_gate, hot_in, hot_down, cold_in, cold_down
):
    tok_dev, model_width = tokens.shape
    top_cold = cold_ids.shape[1]
    data_count = lax.axis_size("dp")
    owner_count = lax.axis_size("expert")
    cold_count = owner_count // 2
    capacity = 5 * tok_dev * top_cold // (4 * cold_count)
    hot_weight = hot_mask.astype(jnp.float32) * hot_gate
    hot_stack = jnp.concatenate([hot_in, hot_down[None]], axis=0)
    ids_flat = cold_ids.reshape(-1)
    one_hot = (ids_flat[:, None] == jnp.arange(cold_count, dtype=jnp.int32)[None, :]).astype(
        jnp.int32
    )
    earlier = jnp.cumsum(one_hot, axis=0) - one_hot
    slot_pos = jnp.sum(one_hot * earlier, axis=1)
    column = ids_flat * capacity + slot_pos
    dispatch = (
        column[:, None] == jnp.arange(cold_count * capacity, dtype=jnp.int32)[None, :]
    ).astype(jnp.bfloat16)
    gates_flat = cold_gate.reshape(-1)
    row_tok = jnp.repeat(tokens, top_cold, axis=0)
    row_cot = (gates_flat[:, None] * jnp.repeat(cotangent, top_cold, axis=0)).astype(jnp.bfloat16)
    stacked = jnp.stack([row_tok, row_cot])
    send_rows = jnp.einsum(
        "rc,srd->scd", dispatch, stacked, preferred_element_type=jnp.float32
    ).astype(jnp.bfloat16)
    send_rows = send_rows.reshape(2, cold_count, capacity, model_width)
    duplicate = jnp.broadcast_to(
        send_rows[:, :, None], (2, cold_count, 2, capacity, model_width)
    ).reshape(2, owner_count, capacity, model_width)
    received = lax.all_to_all(duplicate, "expert", split_axis=1, concat_axis=1, tiled=True)
    row_block = received.reshape(2, owner_count * capacity, model_width)
    out_part, dx_part, cold_grad_in, cold_grad_down = cold_terms(row_block, cold_in, cold_down)
    returned = lax.all_to_all(
        jnp.stack([out_part, dx_part]).reshape(2, owner_count, capacity, model_width),
        "expert",
        split_axis=1,
        concat_axis=1,
        tiled=True,
    )
    summed = jnp.sum(
        returned.astype(jnp.float32).reshape(2, cold_count, 2, capacity, model_width), axis=2
    )
    summed = summed.reshape(2, cold_count * capacity, model_width)
    picked = jnp.take(summed, column, axis=1)
    cold_out = jnp.sum(
        gates_flat.reshape(tok_dev, top_cold, 1)
        * picked[0].reshape(tok_dev, top_cold, model_width),
        axis=1,
    )
    cold_dx = jnp.sum(picked[1].reshape(tok_dev, top_cold, model_width), axis=1)
    own_terms = hot_terms(tokens, cotangent, hot_weight, hot_stack)
    weights = pass_weights(hot_stack)
    first_terms = hot_terms(tokens, cotangent, hot_weight, weights)

    def cycle_turn(hop_count, cycle_state):
        weights, carried, out_sum, dx_sum = cycle_state
        weights = pass_weights(weights)
        carried = pass_grads(carried)
        fresh_terms = hot_terms(tokens, cotangent, hot_weight, weights)
        return (
            weights,
            carried + fresh_terms[2],
            out_sum + fresh_terms[0],
            dx_sum + fresh_terms[1],
        )

    cycle_state = (
        weights,
        first_terms[2],
        own_terms[0] + first_terms[0],
        own_terms[1] + first_terms[1],
    )
    weights, carried, hot_out, hot_dx = lax.fori_loop(2, data_count, cycle_turn, cycle_state)
    hot_grads = pass_grads(carried) + own_terms[2]
    scale_hot = 1.0 / math.sqrt(tok_dev * data_count * owner_count)
    hot_cols = lax.psum_scatter(hot_grads, "expert", scatter_dimension=2, tiled=True) * scale_hot
    scale_cold = 1.0 / math.sqrt(tok_dev * owner_count)
    mixed = (hot_out + cold_out).astype(jnp.bfloat16)
    input_grad = (hot_dx + cold_dx).astype(jnp.bfloat16)
    return (
        mixed,
        input_grad,
        hot_cols[:2],
        hot_cols[2],
        (cold_grad_in * scale_cold).astype(jnp.bfloat16)[None],
        (cold_grad_down * scale_cold).astype(jnp.bfloat16)[None],
    )


def solution(mesh):
    return jax.shard_map(
        body,
        mesh=mesh,
        in_specs=(
            P(("dp", "expert"), None),
            P(("dp", "expert"), None),
            P(("dp", "expert")),
            P(("dp", "expert")),
            P(("dp", "expert"), None),
            P(("dp", "expert"), None),
            P(None, "dp", None),
            P("dp", None),
            P(None, "expert", None),
            P("expert", None),
        ),
        out_specs=(
            P(("dp", "expert"), None),
            P(("dp", "expert"), None),
            P(None, "dp", "expert"),
            P("dp", "expert"),
            P("dp", None, "expert", None),
            P("dp", "expert", None),
        ),
        check_vma=False,
    )
```

profile of v0, /device:TPU:8, one launch (start us, length us, event | category | flops | bytes accessed | tf_op | source)
XLA Modules:
  0.0 713.6 jit_solution(3561489298241170776)
XLA Ops:
  16.4 11.1 %all-to-all-start = ((bf16[2,16,20,2048]{3,0,2,1:T(2,128)(2,1)}), bf16[2,16,20,2048]{3,0,2,1:T(2,128)(2,1)}, u32[]{:S(2)}, u32[]{:S(2)}) async-start(bf16[2,16,20,2048]{3,0,2,1:T(2,128)(2,1)} %bitcast.326), calls=%async_computation | async-start | bytes 5242880 | tf_op jit(solution)/shard_map/all_to_all | solution.py:92
  31.1 8.0 %collective-permute-done.2 = bf16[3,44,2048]{2,1,0:T(8,128)(2,1)S(1)} collective-permute-done((bf16[3,44,2048]{2,1,0:T(8,128)(2,1)S(1)}, bf16[3,44,2048]{2,1,0:T(8,128)(2,1)S(1)}, u32[]{:S(2)}, u32[]{:S(2)}) %collective-permute-start.2) | collective-permute-done | bytes 540704 | tf_op jit(solution)/shard_map/ppermute | solution.py:11
  44.0 47.6 %all-to-all-done = bf16[2,16,20,2048]{3,0,2,1:T(2,128)(2,1)} async-done(((bf16[2,16,20,2048]{3,0,2,1:T(2,128)(2,1)}), bf16[2,16,20,2048]{3,0,2,1:T(2,128)(2,1)}, u32[]{:S(2)}, u32[]{:S(2)}) %all-to-all-start) | async-done | bytes 2621472 | tf_op jit(solution)/shard_map/all_to_all | solution.py:92
  91.6 14.8 %slice_reduce_fusion.1 = (bf16[16,20,2048]{2,1,0:T(8,128)(2,1)}, bf16[16,20,2048]{2,1,0:T(8,128)(2,1)}) fusion(bf16[2,16,20,2048]{3,0,2,1:T(2,128)(2,1)} %all-to-all-done), kind=kLoop, calls=%fused_computation.49 | loop fusion | bytes 5242880 | tf_op jit(solution)/shard_map/slice | solution.py:44
  140.0 414.7 %while.16 = (s32[]{:T(128)}, bf16[3,44,2048]{2,1,0:T(8,128)(2,1)}, f32[3,44,2048]{2,1,0:T(8,128)}, f32[128,2048]{1,0:T(8,128)}, f32[128,2048]{1,0:T(8,128)}, /*i...) while((s32[]{:T(128)}, bf16[3,44,2048]{2,1,0:T(8,128)(2,1)}, ...), condition=%wide.region_1.2_spmd, body=%wide.region_0.0_spmd.sunk | while | flops 208863232 | bytes 40744796 | solution.py:135
  191.6 50.5 %collective-permute-done = bf16[3,44,2048]{2,1,0:T(8,128)(2,1)S(1)} collective-permute-done((bf16[3,44,2048]{2,1,0:T(8,128)(2,1)}, bf16[3,44,2048]{2,1,0:T(8,128)(2,1)S(1)}, u32[]{:S(2)}, u32[]{:S(2)}) %collective-permute-start) | collective-permute-done | bytes 540704 | tf_op jit(solution)/shard_map/while/body/eval_jaxpr/ppermute | solution.py:11
  247.0 7.9 %collective-permute-done.1 = f32[3,44,2048]{2,1,0:T(8,128)} collective-permute-done((f32[3,44,2048]{2,1,0:T(8,128)}, f32[3,44,2048]{2,1,0:T(8,128)}, u32[]{:S(2)}, u32[]{:S(2)}) %collective-permute-start.1) | collective-permute-done | bytes 1081376 | tf_op jit(solution)/shard_map/while/body/eval_jaxpr/ppermute | solution.py:11
  258.4 10.7 %collective-permute-done = bf16[3,44,2048]{2,1,0:T(8,128)(2,1)S(1)} collective-permute-done((bf16[3,44,2048]{2,1,0:T(8,128)(2,1)}, bf16[3,44,2048]{2,1,0:T(8,128)(2,1)S(1)}, u32[]{:S(2)}, u32[]{:S(2)}) %collective-permute-start) | collective-permute-done | bytes 540704 | tf_op jit(solution)/shard_map/while/body/eval_jaxpr/ppermute | solution.py:11
  274.0 7.9 %collective-permute-done.1 = f32[3,44,2048]{2,1,0:T(8,128)} collective-permute-done((f32[3,44,2048]{2,1,0:T(8,128)}, f32[3,44,2048]{2,1,0:T(8,128)}, u32[]{:S(2)}, u32[]{:S(2)}) %collective-permute-start.1) | collective-permute-done | bytes 1081376 | tf_op jit(solution)/shard_map/while/body/eval_jaxpr/ppermute | solution.py:11
  285.4 10.7 %collective-permute-done = bf16[3,44,2048]{2,1,0:T(8,128)(2,1)S(1)} collective-permute-done((bf16[3,44,2048]{2,1,0:T(8,128)(2,1)}, bf16[3,44,2048]{2,1,0:T(8,128)(2,1)S(1)}, u32[]{:S(2)}, u32[]{:S(2)}) %collective-permute-start) | collective-permute-done | bytes 540704 | tf_op jit(solution)/shard_map/while/body/eval_jaxpr/ppermute | solution.py:11
  301.0 7.9 %collective-permute-done.1 = f32[3,44,2048]{2,1,0:T(8,128)} collective-permute-done((f32[3,44,2048]{2,1,0:T(8,128)}, f32[3,44,2048]{2,1,0:T(8,128)}, u32[]{:S(2)}, u32[]{:S(2)}) %collective-permute-start.1) | collective-permute-done | bytes 1081376 | tf_op jit(solution)/shard_map/while/body/eval_jaxpr/ppermute | solution.py:11
  312.5 10.7 %collective-permute-done = bf16[3,44,2048]{2,1,0:T(8,128)(2,1)S(1)} collective-permute-done((bf16[3,44,2048]{2,1,0:T(8,128)(2,1)}, bf16[3,44,2048]{2,1,0:T(8,128)(2,1)S(1)}, u32[]{:S(2)}, u32[]{:S(2)}) %collective-permute-start) | collective-permute-done | bytes 540704 | tf_op jit(solution)/shard_map/while/body/eval_jaxpr/ppermute | solution.py:11
  339.5 10.7 %collective-permute-done = bf16[3,44,2048]{2,1,0:T(8,128)(2,1)S(1)} collective-permute-done((bf16[3,44,2048]{2,1,0:T(8,128)(2,1)}, bf16[3,44,2048]{2,1,0:T(8,128)(2,1)S(1)}, u32[]{:S(2)}, u32[]{:S(2)}) %collective-permute-start) | collective-permute-done | bytes 540704 | tf_op jit(solution)/shard_map/while/body/eval_jaxpr/ppermute | solution.py:11
  366.5 10.7 %collective-permute-done = bf16[3,44,2048]{2,1,0:T(8,128)(2,1)S(1)} collective-permute-done((bf16[3,44,2048]{2,1,0:T(8,128)(2,1)}, bf16[3,44,2048]{2,1,0:T(8,128)(2,1)S(1)}, u32[]{:S(2)}, u32[]{:S(2)}) %collective-permute-start) | collective-permute-done | bytes 540704 | tf_op jit(solution)/shard_map/while/body/eval_jaxpr/ppermute | solution.py:11
  393.5 10.7 %collective-permute-done = bf16[3,44,2048]{2,1,0:T(8,128)(2,1)S(1)} collective-permute-done((bf16[3,44,2048]{2,1,0:T(8,128)(2,1)}, bf16[3,44,2048]{2,1,0:T(8,128)(2,1)S(1)}, u32[]{:S(2)}, u32[]{:S(2)}) %collective-permute-start) | collective-permute-done | bytes 540704 | tf_op jit(solution)/shard_map/while/body/eval_jaxpr/ppermute | solution.py:11
  420.5 10.7 %collective-permute-done = bf16[3,44,2048]{2,1,0:T(8,128)(2,1)S(1)} collective-permute-done((bf16[3,44,2048]{2,1,0:T(8,128)(2,1)}, bf16[3,44,2048]{2,1,0:T(8,128)(2,1)S(1)}, u32[]{:S(2)}, u32[]{:S(2)}) %collective-permute-start) | collective-permute-done | bytes 540704 | tf_op jit(solution)/shard_map/while/body/eval_jaxpr/ppermute | solution.py:11
  447.6 10.7 %collective-permute-done = bf16[3,44,2048]{2,1,0:T(8,128)(2,1)S(1)} collective-permute-done((bf16[3,44,2048]{2,1,0:T(8,128)(2,1)}, bf16[3,44,2048]{2,1,0:T(8,128)(2,1)S(1)}, u32[]{:S(2)}, u32[]{:S(2)}) %collective-permute-start) | collective-permute-done | bytes 540704 | tf_op jit(solution)/shard_map/while/body/eval_jaxpr/ppermute | solution.py:11
  463.2 7.9 %collective-permute-done.1 = f32[3,44,2048]{2,1,0:T(8,128)} collective-permute-done((f32[3,44,2048]{2,1,0:T(8,128)}, f32[3,44,2048]{2,1,0:T(8,128)}, u32[]{:S(2)}, u32[]{:S(2)}) %collective-permute-start.1) | collective-permute-done | bytes 1081376 | tf_op jit(solution)/shard_map/while/body/eval_jaxpr/ppermute | solution.py:11
  474.6 10.7 %collective-permute-done = bf16[3,44,2048]{2,1,0:T(8,128)(2,1)S(1)} collective-permute-done((bf16[3,44,2048]{2,1,0:T(8,128)(2,1)}, bf16[3,44,2048]{2,1,0:T(8,128)(2,1)S(1)}, u32[]{:S(2)}, u32[]{:S(2)}) %collective-permute-start) | collective-permute-done | bytes 540704 | tf_op jit(solution)/shard_map/while/body/eval_jaxpr/ppermute | solution.py:11
  490.2 7.9 %collective-permute-done.1 = f32[3,44,2048]{2,1,0:T(8,128)} collective-permute-done((f32[3,44,2048]{2,1,0:T(8,128)}, f32[3,44,2048]{2,1,0:T(8,128)}, u32[]{:S(2)}, u32[]{:S(2)}) %collective-permute-start.1) | collective-permute-done | bytes 1081376 | tf_op jit(solution)/shard_map/while/body/eval_jaxpr/ppermute | solution.py:11
  501.6 10.7 %collective-permute-done = bf16[3,44,2048]{2,1,0:T(8,128)(2,1)S(1)} collective-permute-done((bf16[3,44,2048]{2,1,0:T(8,128)(2,1)}, bf16[3,44,2048]{2,1,0:T(8,128)(2,1)S(1)}, u32[]{:S(2)}, u32[]{:S(2)}) %collective-permute-start) | collective-permute-done | bytes 540704 | tf_op jit(solution)/shard_map/while/body/eval_jaxpr/ppermute | solution.py:11
  528.6 10.7 %collective-permute-done = bf16[3,44,2048]{2,1,0:T(8,128)(2,1)S(1)} collective-permute-done((bf16[3,44,2048]{2,1,0:T(8,128)(2,1)}, bf16[3,44,2048]{2,1,0:T(8,128)(2,1)S(1)}, u32[]{:S(2)}, u32[]{:S(2)}) %collective-permute-start) | collective-permute-done | bytes 540704 | tf_op jit(solution)/shard_map/while/body/eval_jaxpr/ppermute | solution.py:11
  556.5 16.4 %collective-permute-done.3 = f32[3,44,2048]{2,1,0:T(8,128)S(1)} collective-permute-done((f32[3,44,2048]{2,1,0:T(8,128)}, f32[3,44,2048]{2,1,0:T(8,128)S(1)}, u32[]{:S(2)}, u32[]{:S(2)}) %collective-permute-start.3) | collective-permute-done | bytes 1081376 | tf_op jit(solution)/shard_map/ppermute | solution.py:11
  574.2 105.6 %reduce-scatter.2.cloned.1.call-done = f32[3,44,128]{2,1,0:T(8,128)} async-done(((f32[3,44,2048]{2,1,0:T(8,128)}), f32[3,44,128]{2,1,0:T(8,128)}) %reduce-scatter.2.cloned.1.call-update) | async-done | bytes 67600 | tf_op jit(solution)/shard_map/reduce_scatter | solution.py:138
  (408 shorter events, 286.1 us)
Async XLA Ops:
  16.4 75.2 %all-to-all-start = ((bf16[2,16,20,2048]{3,0,2,1:T(2,128)(2,1)}), bf16[2,16,20,2048]{3,0,2,1:T(2,128)(2,1)}, u32[]{:S(2)}, u32[]{:S(2)}) async-start(bf16[2,16,20,2048]{3,0,2,1:T(2,128)(2,1)} %bitcast.326), calls=%async_computation | async-start | bytes 5242880 | tf_op jit(solution)/shard_map/all_to_all | solution.py:92
  135.5 553.6 %all-to-all-start.1 = ((bf16[2,16,20,2048]{3,0,2,1:T(2,128)(2,1)}), bf16[2,16,20,2048]{3,0,2,1:T(2,128)(2,1)}, u32[]{:S(2)}, u32[]{:S(2)}) async-start(bf16[2,16,20,2048]{3,0,2,1:T(2,128)(2,1)} %copy.31), calls=%async_computation.1 | async-start | bytes 5242880 | tf_op jit(solution)/shard_map/all_to_all | solution.py:95
  139.9 539.8 %reduce-scatter.2.cloned.1.call-start = ((), (), s32[]{:S(2)}) async-start(), calls=%async_computation.3 | async-start | bytes 1253376 | tf_op jit(solution)/shard_map/reduce_scatter | solution.py:138
  140.1 22.3 %collective-permute-start.1 = (f32[3,44,2048]{2,1,0:T(8,128)}, f32[3,44,2048]{2,1,0:T(8,128)}, u32[]{:S(2)}, u32[]{:S(2)}) collective-permute-start(f32[3,44,2048]{2,1,0:T(8,128)} %get-tuple-element.166), channel_id=1, source_target_pairs={{240,0},{0,16},{16,32},{32,48},{48,64},{64,80},{80,96},{96,112},{1... | collective-permute-start | bytes 3244040 | tf_op jit(solution)/shard_map/while/body/eval_jaxpr/ppermute | solution.py:11
  165.0 22.3 %collective-permute-start.1 = (f32[3,44,2048]{2,1,0:T(8,128)}, f32[3,44,2048]{2,1,0:T(8,128)}, u32[]{:S(2)}, u32[]{:S(2)}) collective-permute-start(f32[3,44,2048]{2,1,0:T(8,128)} %get-tuple-element.166), channel_id=1, source_target_pairs={{240,0},{0,16},{16,32},{32,48},{48,64},{64,80},{80,96},{96,112},{1... | collective-permute-start | bytes 3244040 | tf_op jit(solution)/shard_map/while/body/eval_jaxpr/ppermute | solution.py:11
  189.8 52.3 %collective-permute-start = (bf16[3,44,2048]{2,1,0:T(8,128)(2,1)}, bf16[3,44,2048]{2,1,0:T(8,128)(2,1)S(1)}, u32[]{:S(2)}, u32[]{:S(2)}) collective-permute-start(bf16[3,44,2048]{2,1,0:T(8,128)(2,1)} %get-tuple-element.165), channel_id=1, source_target_pairs={{240,0},{0,16},{16,32},{32,48},{48,64},{64,80},{80,96},{96,112},{1... | collective-permute-start | bytes 1622024 | tf_op jit(solution)/shard_map/while/body/eval_jaxpr/ppermute | solution.py:11
  189.9 64.9 %collective-permute-start.1 = (f32[3,44,2048]{2,1,0:T(8,128)}, f32[3,44,2048]{2,1,0:T(8,128)}, u32[]{:S(2)}, u32[]{:S(2)}) collective-permute-start(f32[3,44,2048]{2,1,0:T(8,128)} %get-tuple-element.166), channel_id=1, source_target_pairs={{240,0},{0,16},{16,32},{32,48},{48,64},{64,80},{80,96},{96,112},{1... | collective-permute-start | bytes 3244040 | tf_op jit(solution)/shard_map/while/body/eval_jaxpr/ppermute | solution.py:11
  257.4 11.7 %collective-permute-start = (bf16[3,44,2048]{2,1,0:T(8,128)(2,1)}, bf16[3,44,2048]{2,1,0:T(8,128)(2,1)S(1)}, u32[]{:S(2)}, u32[]{:S(2)}) collective-permute-start(bf16[3,44,2048]{2,1,0:T(8,128)(2,1)} %get-tuple-element.165), channel_id=1, source_target_pairs={{240,0},{0,16},{16,32},{32,48},{48,64},{64,80},{80,96},{96,112},{1... | collective-permute-start | bytes 1622024 | tf_op jit(solution)/shard_map/while/body/eval_jaxpr/ppermute | solution.py:11
  257.5 24.4 %collective-permute-start.1 = (f32[3,44,2048]{2,1,0:T(8,128)}, f32[3,44,2048]{2,1,0:T(8,128)}, u32[]{:S(2)}, u32[]{:S(2)}) collective-permute-start(f32[3,44,2048]{2,1,0:T(8,128)} %get-tuple-element.166), channel_id=1, source_target_pairs={{240,0},{0,16},{16,32},{32,48},{48,64},{64,80},{80,96},{96,112},{1... | collective-permute-start | bytes 3244040 | tf_op jit(solution)/shard_map/while/body/eval_jaxpr/ppermute | solution.py:11
  284.5 24.4 %collective-permute-start.1 = (f32[3,44,2048]{2,1,0:T(8,128)}, f32[3,44,2048]{2,1,0:T(8,128)}, u32[]{:S(2)}, u32[]{:S(2)}) collective-permute-start(f32[3,44,2048]{2,1,0:T(8,128)} %get-tuple-element.166), channel_id=1, source_target_pairs={{240,0},{0,16},{16,32},{32,48},{48,64},{64,80},{80,96},{96,112},{1... | collective-permute-start | bytes 3244040 | tf_op jit(solution)/shard_map/while/body/eval_jaxpr/ppermute | solution.py:11
  311.6 24.4 %collective-permute-start.1 = (f32[3,44,2048]{2,1,0:T(8,128)}, f32[3,44,2048]{2,1,0:T(8,128)}, u32[]{:S(2)}, u32[]{:S(2)}) collective-permute-start(f32[3,44,2048]{2,1,0:T(8,128)} %get-tuple-element.166), channel_id=1, source_target_pairs={{240,0},{0,16},{16,32},{32,48},{48,64},{64,80},{80,96},{96,112},{1... | collective-permute-start | bytes 3244040 | tf_op jit(solution)/shard_map/while/body/eval_jaxpr/ppermute | solution.py:11
  338.6 24.4 %collective-permute-start.1 = (f32[3,44,2048]{2,1,0:T(8,128)}, f32[3,44,2048]{2,1,0:T(8,128)}, u32[]{:S(2)}, u32[]{:S(2)}) collective-permute-start(f32[3,44,2048]{2,1,0:T(8,128)} %get-tuple-element.166), channel_id=1, source_target_pairs={{240,0},{0,16},{16,32},{32,48},{48,64},{64,80},{80,96},{96,112},{1... | collective-permute-start | bytes 3244040 | tf_op jit(solution)/shard_map/while/body/eval_jaxpr/ppermute | solution.py:11
  365.6 24.4 %collective-permute-start.1 = (f32[3,44,2048]{2,1,0:T(8,128)}, f32[3,44,2048]{2,1,0:T(8,128)}, u32[]{:S(2)}, u32[]{:S(2)}) collective-permute-start(f32[3,44,2048]{2,1,0:T(8,128)} %get-tuple-element.166), channel_id=1, source_target_pairs={{240,0},{0,16},{16,32},{32,48},{48,64},{64,80},{80,96},{96,112},{1... | collective-permute-start | bytes 3244040 | tf_op jit(solution)/shard_map/while/body/eval_jaxpr/ppermute | solution.py:11
  392.6 24.4 %collective-permute-start.1 = (f32[3,44,2048]{2,1,0:T(8,128)}, f32[3,44,2048]{2,1,0:T(8,128)}, u32[]{:S(2)}, u32[]{:S(2)}) collective-permute-start(f32[3,44,2048]{2,1,0:T(8,128)} %get-tuple-element.166), channel_id=1, source_target_pairs={{240,0},{0,16},{16,32},{32,48},{48,64},{64,80},{80,96},{96,112},{1... | collective-permute-start | bytes 3244040 | tf_op jit(solution)/shard_map/while/body/eval_jaxpr/ppermute | solution.py:11
  419.6 11.7 %collective-permute-start = (bf16[3,44,2048]{2,1,0:T(8,128)(2,1)}, bf16[3,44,2048]{2,1,0:T(8,128)(2,1)S(1)}, u32[]{:S(2)}, u32[]{:S(2)}) collective-permute-start(bf16[3,44,2048]{2,1,0:T(8,128)(2,1)} %get-tuple-element.165), channel_id=1, source_target_pairs={{240,0},{0,16},{16,32},{32,48},{48,64},{64,80},{80,96},{96,112},{1... | collective-permute-start | bytes 1622024 | tf_op jit(solution)/shard_map/while/body/eval_jaxpr/ppermute | solution.py:11
  419.7 24.4 %collective-permute-start.1 = (f32[3,44,2048]{2,1,0:T(8,128)}, f32[3,44,2048]{2,1,0:T(8,128)}, u32[]{:S(2)}, u32[]{:S(2)}) collective-permute-start(f32[3,44,2048]{2,1,0:T(8,128)} %get-tuple-element.166), channel_id=1, source_target_pairs={{240,0},{0,16},{16,32},{32,48},{48,64},{64,80},{80,96},{96,112},{1... | collective-permute-start | bytes 3244040 | tf_op jit(solution)/shard_map/while/body/eval_jaxpr/ppermute | solution.py:11
  446.6 11.7 %collective-permute-start = (bf16[3,44,2048]{2,1,0:T(8,128)(2,1)}, bf16[3,44,2048]{2,1,0:T(8,128)(2,1)S(1)}, u32[]{:S(2)}, u32[]{:S(2)}) collective-permute-start(bf16[3,44,2048]{2,1,0:T(8,128)(2,1)} %get-tuple-element.165), channel_id=1, source_target_pairs={{240,0},{0,16},{16,32},{32,48},{48,64},{64,80},{80,96},{96,112},{1... | collective-permute-start | bytes 1622024 | tf_op jit(solution)/shard_map/while/body/eval_jaxpr/ppermute | solution.py:11
  446.7 24.4 %collective-permute-start.1 = (f32[3,44,2048]{2,1,0:T(8,128)}, f32[3,44,2048]{2,1,0:T(8,128)}, u32[]{:S(2)}, u32[]{:S(2)}) collective-permute-start(f32[3,44,2048]{2,1,0:T(8,128)} %get-tuple-element.166), channel_id=1, source_target_pairs={{240,0},{0,16},{16,32},{32,48},{48,64},{64,80},{80,96},{96,112},{1... | collective-permute-start | bytes 3244040 | tf_op jit(solution)/shard_map/while/body/eval_jaxpr/ppermute | solution.py:11
  473.6 11.7 %collective-permute-start = (bf16[3,44,2048]{2,1,0:T(8,128)(2,1)}, bf16[3,44,2048]{2,1,0:T(8,128)(2,1)S(1)}, u32[]{:S(2)}, u32[]{:S(2)}) collective-permute-start(bf16[3,44,2048]{2,1,0:T(8,128)(2,1)} %get-tuple-element.165), channel_id=1, source_target_pairs={{240,0},{0,16},{16,32},{32,48},{48,64},{64,80},{80,96},{96,112},{1... | collective-permute-start | bytes 1622024 | tf_op jit(solution)/shard_map/while/body/eval_jaxpr/ppermute | solution.py:11
  473.7 24.4 %collective-permute-start.1 = (f32[3,44,2048]{2,1,0:T(8,128)}, f32[3,44,2048]{2,1,0:T(8,128)}, u32[]{:S(2)}, u32[]{:S(2)}) collective-permute-start(f32[3,44,2048]{2,1,0:T(8,128)} %get-tuple-element.166), channel_id=1, source_target_pairs={{240,0},{0,16},{16,32},{32,48},{48,64},{64,80},{80,96},{96,112},{1... | collective-permute-start | bytes 3244040 | tf_op jit(solution)/shard_map/while/body/eval_jaxpr/ppermute | solution.py:11
  500.6 11.7 %collective-permute-start = (bf16[3,44,2048]{2,1,0:T(8,128)(2,1)}, bf16[3,44,2048]{2,1,0:T(8,128)(2,1)S(1)}, u32[]{:S(2)}, u32[]{:S(2)}) collective-permute-start(bf16[3,44,2048]{2,1,0:T(8,128)(2,1)} %get-tuple-element.165), channel_id=1, source_target_pairs={{240,0},{0,16},{16,32},{32,48},{48,64},{64,80},{80,96},{96,112},{1... | collective-permute-start | bytes 1622024 | tf_op jit(solution)/shard_map/while/body/eval_jaxpr/ppermute | solution.py:11
  500.7 24.4 %collective-permute-start.1 = (f32[3,44,2048]{2,1,0:T(8,128)}, f32[3,44,2048]{2,1,0:T(8,128)}, u32[]{:S(2)}, u32[]{:S(2)}) collective-permute-start(f32[3,44,2048]{2,1,0:T(8,128)} %get-tuple-element.166), channel_id=1, source_target_pairs={{240,0},{0,16},{16,32},{32,48},{48,64},{64,80},{80,96},{96,112},{1... | collective-permute-start | bytes 3244040 | tf_op jit(solution)/shard_map/while/body/eval_jaxpr/ppermute | solution.py:11
  527.7 24.4 %collective-permute-start.1 = (f32[3,44,2048]{2,1,0:T(8,128)}, f32[3,44,2048]{2,1,0:T(8,128)}, u32[]{:S(2)}, u32[]{:S(2)}) collective-permute-start(f32[3,44,2048]{2,1,0:T(8,128)} %get-tuple-element.166), channel_id=1, source_target_pairs={{240,0},{0,16},{16,32},{32,48},{48,64},{64,80},{80,96},{96,112},{1... | collective-permute-start | bytes 3244040 | tf_op jit(solution)/shard_map/while/body/eval_jaxpr/ppermute | solution.py:11
  554.7 18.2 %collective-permute-start.3 = (f32[3,44,2048]{2,1,0:T(8,128)}, f32[3,44,2048]{2,1,0:T(8,128)S(1)}, u32[]{:S(2)}, u32[]{:S(2)}) collective-permute-start(f32[3,44,2048]{2,1,0:T(8,128)} %get-tuple-element.186), channel_id=1, source_target_pairs={{240,0},{0,16},{16,32},{32,48},{48,64},{64,80},{80,96},{96,112},{1... | collective-permute-start | bytes 3244040 | tf_op jit(solution)/shard_map/ppermute | solution.py:11
  (111 other events, 980.1 us)
Sparse Core Ops, SparseCore 0:
  574.2 105.4 reduce-scatter.1
where the time goes:
time: 716 us; the launch traced here: 714 us
  waiting for transfers between devices  472 us (66%)
  matrix products  78.6 us (11%)
  other arithmetic  57.8 us (8%)
  local copies, waits for them, and re-layouts  57 us (8%)
  starting transfers between devices  32 us (4%)
  between operations  14.4 us (2%)
    ppermute x30, waiting for transfers between devices, passed_along(): return lax.ppermute(block, axis, route)  319 us
    reduce_scatter x1, waiting for transfers between devices, body(): lax.psum_scatter(hot_grads, 'expert', scatter_dimension=2, tiled=True)  106 us
    all_to_all x1, waiting for transfers between devices, body(): lax.all_to_all(duplicate, 'expert', split_axis=1, concat_axis=1, tiled=True)  47.6 us
    add x14, other arithmetic, cycle_turn(): carried + fresh_terms[2]  35.6 us
    dot_general x16, matrix products, hot_terms(): jnp.einsum('ktu,td->kud', pre_grad, tokens, preferred_element_type=jnp.fl...  19.9 us
    dot_general x16, matrix products, hot_terms(): jnp.einsum('td,kud->ktu', tokens, weights[:2], preferred_element_type=jnp...  19.4 us
    ppermute x30, starting transfers between devices, passed_along(): return lax.ppermute(block, axis, route)  16.4 us
    slice x1, local copies, waits for them, and re-layouts, cold_terms(): row_block[0]  14.8 us
  transfers between devices with their start and end apart: 33, of which 32 were waited for; matrix products, arithmetic and copies ran while one was open for 17% of the time, Pallas kernels for 0%

commit v1 on v0

--- a/solution.py
+++ b/solution.py
@@ -1,8 +1,20 @@
+import functools
 import math
 import jax
 import jax.numpy as jnp
 from jax import lax
 from jax.sharding import PartitionSpec as P
+from jax.lax import all_to_all, axis_size
+
+
+def define_the_targets(x_local, array_dim, dim_at):
+    extra = all_to_all(
+        jnp.stack(jnp.split(x_local, axis_size("expert"), array_dim)), "expert", 0, 0
+    )
+    return jnp.concatenate(extra, dim_at)
+
+
+use_the_vectors = functools.partial(define_the_targets, array_dim=1, dim_at=1)
 
 
 def passed_along(block, axis, distance):
@@ -89,7 +101,7 @@
     duplicate = jnp.broadcast_to(
         send_rows[:, :, None], (2, cold_count, 2, capacity, model_width)
     ).reshape(2, owner_count, capacity, model_width)
-    received = lax.all_to_all(duplicate, "expert", split_axis=1, concat_axis=1, tiled=True)
+    received = use_the_vectors(duplicate)
     row_block = received.reshape(2, owner_count * capacity, model_width)
     out_part, dx_part, cold_grad_in, cold_grad_down = cold_terms(row_block, cold_in, cold_down)
     returned = lax.all_to_all(

time: 716 us -> 728 us (1.017)
  local copies, waits for them, and re-layouts: 57 us -> 67.9 us
    unnamed x38 -> x53, local copies, waits for them, and re-layouts: 1.92 us -> 13.6 us
where the time goes in v1:
time: 728 us; the launch traced here: 726 us
  waiting for transfers between devices  472 us (65%)
  matrix products  79.3 us (11%)
  local copies, waits for them, and re-layouts  67.9 us (9%)
  other arithmetic  57.8 us (8%)
  starting transfers between devices  32.7 us (4%)
  between operations  14.4 us (2%)
    ppermute x30, waiting for transfers between devices, passed_along(): return lax.ppermute(block, axis, route)  319 us
    reduce_scatter x1, waiting for transfers between devices, body(): lax.psum_scatter(hot_grads, 'expert', scatter_dimension=2, tiled=True)  106 us
    all_to_all x1, waiting for transfers between devices, define_the_targets(): all_to_all(jnp.stack(jnp.split(x_local, axis_size('expert'), array_dim)),...  47.6 us
    add x14, other arithmetic, cycle_turn(): carried + fresh_terms[2]  35.6 us
    dot_general x16, matrix products, hot_terms(): jnp.einsum('td,kud->ktu', tokens, weights[:2], preferred_element_type=jnp...  20.4 us
    dot_general x16, matrix products, hot_terms(): jnp.einsum('ktu,td->kud', pre_grad, tokens, preferred_element_type=jnp.fl...  18.7 us
    ppermute x30, starting transfers between devices, passed_along(): return lax.ppermute(block, axis, route)  17 us
    slice x1, local copies, waits for them, and re-layouts, cold_terms(): row_block[0]  14.8 us
  transfers between devices with their start and end apart: 33, of which 32 were waited for; matrix products, arithmetic and copies ran while one was open for 17% of the time, Pallas kernels for 0%

profile of v1, /device:TPU:8, one launch (start us, length us, event | category | flops | bytes accessed | tf_op | source)
XLA Modules:
  0.0 725.7 jit_solution(1243893202386198665)
XLA Ops:
  28.4 11.2 %all-to-all-start = ((bf16[16,2,1,20,2048]{4,1,3,2,0:T(2,128)(2,1)}), bf16[16,2,1,20,2048]{4,1,3,2,0:T(2,128)(2,1)}, u32[]{:S(2)}, u32[]{:S(2)}) async-start(bf16[16,2,1,20,2048]{4,1,3,2,0:T(2,128)(2,1)} %fusion.59), calls=%async_computation | async-start | bytes 5242880 | tf_op jit(solution)/shard_map/all_to_all | solution.py:11
  56.1 47.6 %all-to-all-done = bf16[16,2,1,20,2048]{4,1,3,2,0:T(2,128)(2,1)} async-done(((bf16[16,2,1,20,2048]{4,1,3,2,0:T(2,128)(2,1)}), bf16[16,2,1,20,2048]{4,1,3,2,0:T(2,128)(2,1)}, u32[]{:S(2)}, u32[]{:S(2)}) %all-to-all-start) | async-done | bytes 2621472 | tf_op jit(solution)/shard_map/all_to_all | solution.py:11
  103.7 14.8 %slice_reduce_fusion.1 = (bf16[16,20,2048]{2,1,0:T(8,128)(2,1)}, bf16[16,20,2048]{2,1,0:T(8,128)(2,1)}) fusion(bf16[2,16,1,20,2048]{4,0,3,2,1:T(2,128)(2,1)} %bitcast.55), kind=kLoop, calls=%fused_computation.49 | loop fusion | bytes 5242880 | tf_op jit(solution)/shard_map/slice | solution.py:56
  152.1 414.6 %while.16 = (s32[]{:T(128)}, bf16[3,44,2048]{2,1,0:T(8,128)(2,1)}, f32[3,44,2048]{2,1,0:T(8,128)}, f32[128,2048]{1,0:T(8,128)}, f32[128,2048]{1,0:T(8,128)}, /*i...) while((s32[]{:T(128)}, bf16[3,44,2048]{2,1,0:T(8,128)(2,1)}, ...), condition=%wide.region_1.2_spmd, body=%wide.region_0.0_spmd.sunk | while | flops 208863232 | bytes 40744796 | solution.py:147
  166.5 8.0 %collective-permute-done.1 = f32[3,44,2048]{2,1,0:T(8,128)} collective-permute-done((f32[3,44,2048]{2,1,0:T(8,128)}, f32[3,44,2048]{2,1,0:T(8,128)}, u32[]{:S(2)}, u32[]{:S(2)}) %collective-permute-start.1) | collective-permute-done | bytes 1081376 | tf_op jit(solution)/shard_map/while/body/eval_jaxpr/ppermute | solution.py:23
  191.4 8.0 %collective-permute-done.1 = f32[3,44,2048]{2,1,0:T(8,128)} collective-permute-done((f32[3,44,2048]{2,1,0:T(8,128)}, f32[3,44,2048]{2,1,0:T(8,128)}, u32[]{:S(2)}, u32[]{:S(2)}) %collective-permute-start.1) | collective-permute-done | bytes 1081376 | tf_op jit(solution)/shard_map/while/body/eval_jaxpr/ppermute | solution.py:23
  203.7 50.4 %collective-permute-done = bf16[3,44,2048]{2,1,0:T(8,128)(2,1)S(1)} collective-permute-done((bf16[3,44,2048]{2,1,0:T(8,128)(2,1)}, bf16[3,44,2048]{2,1,0:T(8,128)(2,1)S(1)}, u32[]{:S(2)}, u32[]{:S(2)}) %collective-permute-start) | collective-permute-done | bytes 540704 | tf_op jit(solution)/shard_map/while/body/eval_jaxpr/ppermute | solution.py:23
  270.5 10.7 %collective-permute-done = bf16[3,44,2048]{2,1,0:T(8,128)(2,1)S(1)} collective-permute-done((bf16[3,44,2048]{2,1,0:T(8,128)(2,1)}, bf16[3,44,2048]{2,1,0:T(8,128)(2,1)S(1)}, u32[]{:S(2)}, u32[]{:S(2)}) %collective-permute-start) | collective-permute-done | bytes 540704 | tf_op jit(solution)/shard_map/while/body/eval_jaxpr/ppermute | solution.py:23
  297.5 10.7 %collective-permute-done = bf16[3,44,2048]{2,1,0:T(8,128)(2,1)S(1)} collective-permute-done((bf16[3,44,2048]{2,1,0:T(8,128)(2,1)}, bf16[3,44,2048]{2,1,0:T(8,128)(2,1)S(1)}, u32[]{:S(2)}, u32[]{:S(2)}) %collective-permute-start) | collective-permute-done | bytes 540704 | tf_op jit(solution)/shard_map/while/body/eval_jaxpr/ppermute | solution.py:23
  324.6 10.7 %collective-permute-done = bf16[3,44,2048]{2,1,0:T(8,128)(2,1)S(1)} collective-permute-done((bf16[3,44,2048]{2,1,0:T(8,128)(2,1)}, bf16[3,44,2048]{2,1,0:T(8,128)(2,1)S(1)}, u32[]{:S(2)}, u32[]{:S(2)}) %collective-permute-start) | collective-permute-done | bytes 540704 | tf_op jit(solution)/shard_map/while/body/eval_jaxpr/ppermute | solution.py:23
  340.0 8.0 %collective-permute-done.1 = f32[3,44,2048]{2,1,0:T(8,128)} collective-permute-done((f32[3,44,2048]{2,1,0:T(8,128)}, f32[3,44,2048]{2,1,0:T(8,128)}, u32[]{:S(2)}, u32[]{:S(2)}) %collective-permute-start.1) | collective-permute-done | bytes 1081376 | tf_op jit(solution)/shard_map/while/body/eval_jaxpr/ppermute | solution.py:23
  351.6 10.7 %collective-permute-done = bf16[3,44,2048]{2,1,0:T(8,128)(2,1)S(1)} collective-permute-done((bf16[3,44,2048]{2,1,0:T(8,128)(2,1)}, bf16[3,44,2048]{2,1,0:T(8,128)(2,1)S(1)}, u32[]{:S(2)}, u32[]{:S(2)}) %collective-permute-start) | collective-permute-done | bytes 540704 | tf_op jit(solution)/shard_map/while/body/eval_jaxpr/ppermute | solution.py:23
  367.0 8.0 %collective-permute-done.1 = f32[3,44,2048]{2,1,0:T(8,128)} collective-permute-done((f32[3,44,2048]{2,1,0:T(8,128)}, f32[3,44,2048]{2,1,0:T(8,128)}, u32[]{:S(2)}, u32[]{:S(2)}) %collective-permute-start.1) | collective-permute-done | bytes 1081376 | tf_op jit(solution)/shard_map/while/body/eval_jaxpr/ppermute | solution.py:23
  378.6 10.7 %collective-permute-done = bf16[3,44,2048]{2,1,0:T(8,128)(2,1)S(1)} collective-permute-done((bf16[3,44,2048]{2,1,0:T(8,128)(2,1)}, bf16[3,44,2048]{2,1,0:T(8,128)(2,1)S(1)}, u32[]{:S(2)}, u32[]{:S(2)}) %collective-permute-start) | collective-permute-done | bytes 540704 | tf_op jit(solution)/shard_map/while/body/eval_jaxpr/ppermute | solution.py:23
  394.0 8.0 %collective-permute-done.1 = f32[3,44,2048]{2,1,0:T(8,128)} collective-permute-done((f32[3,44,2048]{2,1,0:T(8,128)}, f32[3,44,2048]{2,1,0:T(8,128)}, u32[]{:S(2)}, u32[]{:S(2)}) %collective-permute-start.1) | collective-permute-done | bytes 1081376 | tf_op jit(solution)/shard_map/while/body/eval_jaxpr/ppermute | solution.py:23
  405.6 10.7 %collective-permute-done = bf16[3,44,2048]{2,1,0:T(8,128)(2,1)S(1)} collective-permute-done((bf16[3,44,2048]{2,1,0:T(8,128)(2,1)}, bf16[3,44,2048]{2,1,0:T(8,128)(2,1)S(1)}, u32[]{:S(2)}, u32[]{:S(2)}) %collective-permute-start) | collective-permute-done | bytes 540704 | tf_op jit(solution)/shard_map/while/body/eval_jaxpr/ppermute | solution.py:23
  421.0 8.0 %collective-permute-done.1 = f32[3,44,2048]{2,1,0:T(8,128)} collective-permute-done((f32[3,44,2048]{2,1,0:T(8,128)}, f32[3,44,2048]{2,1,0:T(8,128)}, u32[]{:S(2)}, u32[]{:S(2)}) %collective-permute-start.1) | collective-permute-done | bytes 1081376 | tf_op jit(solution)/shard_map/while/body/eval_jaxpr/ppermute | solution.py:23
  432.6 10.7 %collective-permute-done = bf16[3,44,2048]{2,1,0:T(8,128)(2,1)S(1)} collective-permute-done((bf16[3,44,2048]{2,1,0:T(8,128)(2,1)}, bf16[3,44,2048]{2,1,0:T(8,128)(2,1)S(1)}, u32[]{:S(2)}, u32[]{:S(2)}) %collective-permute-start) | collective-permute-done | bytes 540704 | tf_op jit(solution)/shard_map/while/body/eval_jaxpr/ppermute | solution.py:23
  459.7 10.7 %collective-permute-done = bf16[3,44,2048]{2,1,0:T(8,128)(2,1)S(1)} collective-permute-done((bf16[3,44,2048]{2,1,0:T(8,128)(2,1)}, bf16[3,44,2048]{2,1,0:T(8,128)(2,1)S(1)}, u32[]{:S(2)}, u32[]{:S(2)}) %collective-permute-start) | collective-permute-done | bytes 540704 | tf_op jit(solution)/shard_map/while/body/eval_jaxpr/ppermute | solution.py:23
  486.7 10.7 %collective-permute-done = bf16[3,44,2048]{2,1,0:T(8,128)(2,1)S(1)} collective-permute-done((bf16[3,44,2048]{2,1,0:T(8,128)(2,1)}, bf16[3,44,2048]{2,1,0:T(8,128)(2,1)S(1)}, u32[]{:S(2)}, u32[]{:S(2)}) %collective-permute-start) | collective-permute-done | bytes 540704 | tf_op jit(solution)/shard_map/while/body/eval_jaxpr/ppermute | solution.py:23
  513.7 10.7 %collective-permute-done = bf16[3,44,2048]{2,1,0:T(8,128)(2,1)S(1)} collective-permute-done((bf16[3,44,2048]{2,1,0:T(8,128)(2,1)}, bf16[3,44,2048]{2,1,0:T(8,128)(2,1)S(1)}, u32[]{:S(2)}, u32[]{:S(2)}) %collective-permute-start) | collective-permute-done | bytes 540704 | tf_op jit(solution)/shard_map/while/body/eval_jaxpr/ppermute | solution.py:23
  540.7 10.7 %collective-permute-done = bf16[3,44,2048]{2,1,0:T(8,128)(2,1)S(1)} collective-permute-done((bf16[3,44,2048]{2,1,0:T(8,128)(2,1)}, bf16[3,44,2048]{2,1,0:T(8,128)(2,1)S(1)}, u32[]{:S(2)}, u32[]{:S(2)}) %collective-permute-start) | collective-permute-done | bytes 540704 | tf_op jit(solution)/shard_map/while/body/eval_jaxpr/ppermute | solution.py:23
  568.6 16.4 %collective-permute-done.3 = f32[3,44,2048]{2,1,0:T(8,128)S(1)} collective-permute-done((f32[3,44,2048]{2,1,0:T(8,128)}, f32[3,44,2048]{2,1,0:T(8,128)S(1)}, u32[]{:S(2)}, u32[]{:S(2)}) %collective-permute-start.3) | collective-permute-done | bytes 1081376 | tf_op jit(solution)/shard_map/ppermute | solution.py:23
  586.2 105.7 %reduce-scatter.2.cloned.1.call-done = f32[3,44,128]{2,1,0:T(8,128)} async-done(((f32[3,44,2048]{2,1,0:T(8,128)}), f32[3,44,128]{2,1,0:T(8,128)}) %reduce-scatter.2.cloned.1.call-update) | async-done | bytes 67600 | tf_op jit(solution)/shard_map/reduce_scatter | solution.py:150
  (424 shorter events, 298.3 us)
Async XLA Ops:
  28.4 75.3 %all-to-all-start = ((bf16[16,2,1,20,2048]{4,1,3,2,0:T(2,128)(2,1)}), bf16[16,2,1,20,2048]{4,1,3,2,0:T(2,128)(2,1)}, u32[]{:S(2)}, u32[]{:S(2)}) async-start(bf16[16,2,1,20,2048]{4,1,3,2,0:T(2,128)(2,1)} %fusion.59), calls=%async_computation | async-start | bytes 5242880 | tf_op jit(solution)/shard_map/all_to_all | solution.py:11
  147.6 553.5 %all-to-all-start.1 = ((bf16[2,16,20,2048]{3,0,2,1:T(2,128)(2,1)}), bf16[2,16,20,2048]{3,0,2,1:T(2,128)(2,1)}, u32[]{:S(2)}, u32[]{:S(2)}) async-start(bf16[2,16,20,2048]{3,0,2,1:T(2,128)(2,1)} %copy.62), calls=%async_computation.1 | async-start | bytes 5242880 | tf_op jit(solution)/shard_map/all_to_all | solution.py:107
  152.1 539.8 %reduce-scatter.2.cloned.1.call-start = ((), (), s32[]{:S(2)}) async-start(), calls=%async_computation.3 | async-start | bytes 1253376 | tf_op jit(solution)/shard_map/reduce_scatter | solution.py:150
  152.2 22.3 %collective-permute-start.1 = (f32[3,44,2048]{2,1,0:T(8,128)}, f32[3,44,2048]{2,1,0:T(8,128)}, u32[]{:S(2)}, u32[]{:S(2)}) collective-permute-start(f32[3,44,2048]{2,1,0:T(8,128)} %get-tuple-element.166), channel_id=1, source_target_pairs={{240,0},{0,16},{16,32},{32,48},{48,64},{64,80},{80,96},{96,112},{1... | collective-permute-start | bytes 3244040 | tf_op jit(solution)/shard_map/while/body/eval_jaxpr/ppermute | solution.py:23
  177.1 22.3 %collective-permute-start.1 = (f32[3,44,2048]{2,1,0:T(8,128)}, f32[3,44,2048]{2,1,0:T(8,128)}, u32[]{:S(2)}, u32[]{:S(2)}) collective-permute-start(f32[3,44,2048]{2,1,0:T(8,128)} %get-tuple-element.166), channel_id=1, source_target_pairs={{240,0},{0,16},{16,32},{32,48},{48,64},{64,80},{80,96},{96,112},{1... | collective-permute-start | bytes 3244040 | tf_op jit(solution)/shard_map/while/body/eval_jaxpr/ppermute | solution.py:23
  202.0 52.2 %collective-permute-start = (bf16[3,44,2048]{2,1,0:T(8,128)(2,1)}, bf16[3,44,2048]{2,1,0:T(8,128)(2,1)S(1)}, u32[]{:S(2)}, u32[]{:S(2)}) collective-permute-start(bf16[3,44,2048]{2,1,0:T(8,128)(2,1)} %get-tuple-element.165), channel_id=1, source_target_pairs={{240,0},{0,16},{16,32},{32,48},{48,64},{64,80},{80,96},{96,112},{1... | collective-permute-start | bytes 1622024 | tf_op jit(solution)/shard_map/while/body/eval_jaxpr/ppermute | solution.py:23
  202.1 64.8 %collective-permute-start.1 = (f32[3,44,2048]{2,1,0:T(8,128)}, f32[3,44,2048]{2,1,0:T(8,128)}, u32[]{:S(2)}, u32[]{:S(2)}) collective-permute-start(f32[3,44,2048]{2,1,0:T(8,128)} %get-tuple-element.166), channel_id=1, source_target_pairs={{240,0},{0,16},{16,32},{32,48},{48,64},{64,80},{80,96},{96,112},{1... | collective-permute-start | bytes 3244040 | tf_op jit(solution)/shard_map/while/body/eval_jaxpr/ppermute | solution.py:23
  269.5 11.7 %collective-permute-start = (bf16[3,44,2048]{2,1,0:T(8,128)(2,1)}, bf16[3,44,2048]{2,1,0:T(8,128)(2,1)S(1)}, u32[]{:S(2)}, u32[]{:S(2)}) collective-permute-start(bf16[3,44,2048]{2,1,0:T(8,128)(2,1)} %get-tuple-element.165), channel_id=1, source_target_pairs={{240,0},{0,16},{16,32},{32,48},{48,64},{64,80},{80,96},{96,112},{1... | collective-permute-start | bytes 1622024 | tf_op jit(solution)/shard_map/while/body/eval_jaxpr/ppermute | solution.py:23
  269.6 24.4 %collective-permute-start.1 = (f32[3,44,2048]{2,1,0:T(8,128)}, f32[3,44,2048]{2,1,0:T(8,128)}, u32[]{:S(2)}, u32[]{:S(2)}) collective-permute-start(f32[3,44,2048]{2,1,0:T(8,128)} %get-tuple-element.166), channel_id=1, source_target_pairs={{240,0},{0,16},{16,32},{32,48},{48,64},{64,80},{80,96},{96,112},{1... | collective-permute-start | bytes 3244040 | tf_op jit(solution)/shard_map/while/body/eval_jaxpr/ppermute | solution.py:23
  296.5 11.7 %collective-permute-start = (bf16[3,44,2048]{2,1,0:T(8,128)(2,1)}, bf16[3,44,2048]{2,1,0:T(8,128)(2,1)S(1)}, u32[]{:S(2)}, u32[]{:S(2)}) collective-permute-start(bf16[3,44,2048]{2,1,0:T(8,128)(2,1)} %get-tuple-element.165), channel_id=1, source_target_pairs={{240,0},{0,16},{16,32},{32,48},{48,64},{64,80},{80,96},{96,112},{1... | collective-permute-start | bytes 1622024 | tf_op jit(solution)/shard_map/while/body/eval_jaxpr/ppermute | solution.py:23
  296.6 24.4 %collective-permute-start.1 = (f32[3,44,2048]{2,1,0:T(8,128)}, f32[3,44,2048]{2,1,0:T(8,128)}, u32[]{:S(2)}, u32[]{:S(2)}) collective-permute-start(f32[3,44,2048]{2,1,0:T(8,128)} %get-tuple-element.166), channel_id=1, source_target_pairs={{240,0},{0,16},{16,32},{32,48},{48,64},{64,80},{80,96},{96,112},{1... | collective-permute-start | bytes 3244040 | tf_op jit(solution)/shard_map/while/body/eval_jaxpr/ppermute | solution.py:23
  323.5 11.7 %collective-permute-start = (bf16[3,44,2048]{2,1,0:T(8,128)(2,1)}, bf16[3,44,2048]{2,1,0:T(8,128)(2,1)S(1)}, u32[]{:S(2)}, u32[]{:S(2)}) collective-permute-start(bf16[3,44,2048]{2,1,0:T(8,128)(2,1)} %get-tuple-element.165), channel_id=1, source_target_pairs={{240,0},{0,16},{16,32},{32,48},{48,64},{64,80},{80,96},{96,112},{1... | collective-permute-start | bytes 1622024 | tf_op jit(solution)/shard_map/while/body/eval_jaxpr/ppermute | solution.py:23
  323.6 24.4 %collective-permute-start.1 = (f32[3,44,2048]{2,1,0:T(8,128)}, f32[3,44,2048]{2,1,0:T(8,128)}, u32[]{:S(2)}, u32[]{:S(2)}) collective-permute-start(f32[3,44,2048]{2,1,0:T(8,128)} %get-tuple-element.166), channel_id=1, source_target_pairs={{240,0},{0,16},{16,32},{32,48},{48,64},{64,80},{80,96},{96,112},{1... | collective-permute-start | bytes 3244040 | tf_op jit(solution)/shard_map/while/body/eval_jaxpr/ppermute | solution.py:23
  350.5 11.7 %collective-permute-start = (bf16[3,44,2048]{2,1,0:T(8,128)(2,1)}, bf16[3,44,2048]{2,1,0:T(8,128)(2,1)S(1)}, u32[]{:S(2)}, u32[]{:S(2)}) collective-permute-start(bf16[3,44,2048]{2,1,0:T(8,128)(2,1)} %get-tuple-element.165), channel_id=1, source_target_pairs={{240,0},{0,16},{16,32},{32,48},{48,64},{64,80},{80,96},{96,112},{1... | collective-permute-start | bytes 1622024 | tf_op jit(solution)/shard_map/while/body/eval_jaxpr/ppermute | solution.py:23
  350.6 24.4 %collective-permute-start.1 = (f32[3,44,2048]{2,1,0:T(8,128)}, f32[3,44,2048]{2,1,0:T(8,128)}, u32[]{:S(2)}, u32[]{:S(2)}) collective-permute-start(f32[3,44,2048]{2,1,0:T(8,128)} %get-tuple-element.166), channel_id=1, source_target_pairs={{240,0},{0,16},{16,32},{32,48},{48,64},{64,80},{80,96},{96,112},{1... | collective-permute-start | bytes 3244040 | tf_op jit(solution)/shard_map/while/body/eval_jaxpr/ppermute | solution.py:23
  377.6 24.4 %collective-permute-start.1 = (f32[3,44,2048]{2,1,0:T(8,128)}, f32[3,44,2048]{2,1,0:T(8,128)}, u32[]{:S(2)}, u32[]{:S(2)}) collective-permute-start(f32[3,44,2048]{2,1,0:T(8,128)} %get-tuple-element.166), channel_id=1, source_target_pairs={{240,0},{0,16},{16,32},{32,48},{48,64},{64,80},{80,96},{96,112},{1... | collective-permute-start | bytes 3244040 | tf_op jit(solution)/shard_map/while/body/eval_jaxpr/ppermute | solution.py:23
  404.7 24.4 %collective-permute-start.1 = (f32[3,44,2048]{2,1,0:T(8,128)}, f32[3,44,2048]{2,1,0:T(8,128)}, u32[]{:S(2)}, u32[]{:S(2)}) collective-permute-start(f32[3,44,2048]{2,1,0:T(8,128)} %get-tuple-element.166), channel_id=1, source_target_pairs={{240,0},{0,16},{16,32},{32,48},{48,64},{64,80},{80,96},{96,112},{1... | collective-permute-start | bytes 3244040 | tf_op jit(solution)/shard_map/while/body/eval_jaxpr/ppermute | solution.py:23
  431.7 24.4 %collective-permute-start.1 = (f32[3,44,2048]{2,1,0:T(8,128)}, f32[3,44,2048]{2,1,0:T(8,128)}, u32[]{:S(2)}, u32[]{:S(2)}) collective-permute-start(f32[3,44,2048]{2,1,0:T(8,128)} %get-tuple-element.166), channel_id=1, source_target_pairs={{240,0},{0,16},{16,32},{32,48},{48,64},{64,80},{80,96},{96,112},{1... | collective-permute-start | bytes 3244040 | tf_op jit(solution)/shard_map/while/body/eval_jaxpr/ppermute | solution.py:23
  458.7 24.4 %collective-permute-start.1 = (f32[3,44,2048]{2,1,0:T(8,128)}, f32[3,44,2048]{2,1,0:T(8,128)}, u32[]{:S(2)}, u32[]{:S(2)}) collective-permute-start(f32[3,44,2048]{2,1,0:T(8,128)} %get-tuple-element.166), channel_id=1, source_target_pairs={{240,0},{0,16},{16,32},{32,48},{48,64},{64,80},{80,96},{96,112},{1... | collective-permute-start | bytes 3244040 | tf_op jit(solution)/shard_map/while/body/eval_jaxpr/ppermute | solution.py:23
  485.7 24.4 %collective-permute-start.1 = (f32[3,44,2048]{2,1,0:T(8,128)}, f32[3,44,2048]{2,1,0:T(8,128)}, u32[]{:S(2)}, u32[]{:S(2)}) collective-permute-start(f32[3,44,2048]{2,1,0:T(8,128)} %get-tuple-element.166), channel_id=1, source_target_pairs={{240,0},{0,16},{16,32},{32,48},{48,64},{64,80},{80,96},{96,112},{1... | collective-permute-start | bytes 3244040 | tf_op jit(solution)/shard_map/while/body/eval_jaxpr/ppermute | solution.py:23
  512.7 11.7 %collective-permute-start = (bf16[3,44,2048]{2,1,0:T(8,128)(2,1)}, bf16[3,44,2048]{2,1,0:T(8,128)(2,1)S(1)}, u32[]{:S(2)}, u32[]{:S(2)}) collective-permute-start(bf16[3,44,2048]{2,1,0:T(8,128)(2,1)} %get-tuple-element.165), channel_id=1, source_target_pairs={{240,0},{0,16},{16,32},{32,48},{48,64},{64,80},{80,96},{96,112},{1... | collective-permute-start | bytes 1622024 | tf_op jit(solution)/shard_map/while/body/eval_jaxpr/ppermute | solution.py:23
  512.8 24.4 %collective-permute-start.1 = (f32[3,44,2048]{2,1,0:T(8,128)}, f32[3,44,2048]{2,1,0:T(8,128)}, u32[]{:S(2)}, u32[]{:S(2)}) collective-permute-start(f32[3,44,2048]{2,1,0:T(8,128)} %get-tuple-element.166), channel_id=1, source_target_pairs={{240,0},{0,16},{16,32},{32,48},{48,64},{64,80},{80,96},{96,112},{1... | collective-permute-start | bytes 3244040 | tf_op jit(solution)/shard_map/while/body/eval_jaxpr/ppermute | solution.py:23
  539.8 24.4 %collective-permute-start.1 = (f32[3,44,2048]{2,1,0:T(8,128)}, f32[3,44,2048]{2,1,0:T(8,128)}, u32[]{:S(2)}, u32[]{:S(2)}) collective-permute-start(f32[3,44,2048]{2,1,0:T(8,128)} %get-tuple-element.166), channel_id=1, source_target_pairs={{240,0},{0,16},{16,32},{32,48},{48,64},{64,80},{80,96},{96,112},{1... | collective-permute-start | bytes 3244040 | tf_op jit(solution)/shard_map/while/body/eval_jaxpr/ppermute | solution.py:23
  566.7 18.2 %collective-permute-start.3 = (f32[3,44,2048]{2,1,0:T(8,128)}, f32[3,44,2048]{2,1,0:T(8,128)S(1)}, u32[]{:S(2)}, u32[]{:S(2)}) collective-permute-start(f32[3,44,2048]{2,1,0:T(8,128)} %get-tuple-element.186), channel_id=1, source_target_pairs={{240,0},{0,16},{16,32},{32,48},{48,64},{64,80},{80,96},{96,112},{1... | collective-permute-start | bytes 3244040 | tf_op jit(solution)/shard_map/ppermute | solution.py:23
  (111 other events, 1249.9 us)
Sparse Core Ops, SparseCore 0:
  586.3 105.5 reduce-scatter.1
